TPU v7x, 32 devices: a whole 2x2x4 slice. The times are simulated.
32 devices in a mesh: dp: 2 (over x), expert: 4 (over y, core), tensor: 4 (over z).
Axes of the slice: x: 2, y: 2, z: 4, core: 2. Of those that a mesh axis runs over, the one named last changes fastest.
Arguments:
- output_grad: bfloat16 [2048, 4096], P(('dp', 'expert'), 'tensor'), may hold values from -6 to 6
- expert_ids: int32 [2048, 2], P(('dp', 'expert')), may hold values from 0 to 3, all different within a row; in each aligned block of 256 rows (0 to 255, 256 to 511, ...) at most 192 rows name the same one
- router_weights: bfloat16 [2048, 2], P(('dp', 'expert')), may hold values from 0.099609375 to 0.8984375
- gate_preact: bfloat16 [4, 1536, 14336], P('expert', 'dp', 'tensor'), may hold values from -6 to 6
- up_preact: bfloat16 [4, 1536, 14336], P('expert', 'dp', 'tensor'), may hold values from -6 to 6
- down_weight: bfloat16 [4, 14336, 4096], P('expert', 'tensor', 'dp'), may hold values from -0.046875 to 0.046875
Outputs:
- gate_preact_grad: bfloat16 [4, 1536, 14336], P('expert', 'dp', 'tensor')
- up_preact_grad: bfloat16 [4, 1536, 14336], P('expert', 'dp', 'tensor')
- down_grad: bfloat16 [4, 14336, 4096], P('expert', 'tensor', 'dp')
- router_grad: float32 [2048, 2], P(('dp', 'expert'))
Inputs may be any that keep to these rules, and one draw needn't show every extreme that they name: `expert_ids`: the ids of one token differ. Among the 256 rows of one device no expert is named by more than 192 rows, and in every draw some expert is named by exactly 192 rows of some device.
All inputs are finite; a program needn't handle non-finite values.
Results may differ from a plain program's by a relative error of at most 0.007.
Values may be sent and summed in bfloat16 or wider, within the bound.
No kernel may reach another device: no remote copies, remote signals or barrier semaphores. Data moves between devices by JAX's collectives and lax.ppermute only.
A program may use at most 192 MiB of HBM per device.

v0:
```python
import jax
import jax.numpy as jnp
from jax import lax
from jax.sharding import PartitionSpec as P


def silu_parts(values):
    sigma = jax.nn.sigmoid(values)
    return (values * sigma, sigma * (1.0 + values * (1.0 - sigma)))


def local(output_grad, expert_ids, router_weights, gate_preact, up_preact, down_weight):
    expert_count = lax.axis_size("expert")
    tokens_here = expert_ids.shape[0]
    choices_each = expert_ids.shape[1]
    capacity = gate_preact.shape[1] // expert_count
    flat_ids = expert_ids.reshape(-1)
    one_hot = (flat_ids[:, None] == jnp.arange(expert_count, dtype=jnp.int32)).astype(jnp.int32)
    earlier = jnp.cumsum(one_hot, axis=0) - one_hot
    slot_index = jnp.sum(earlier * one_hot, axis=1)
    target = (flat_ids * capacity + slot_index).reshape(tokens_here, choices_each)
    columns = jnp.arange(expert_count * capacity, dtype=jnp.int32)
    matches = [target[:, which][:, None] == columns[None, :] for which in range(choices_each)]
    selector = jnp.zeros((tokens_here, expert_count * capacity), jnp.bfloat16)
    gate_table = jnp.zeros((tokens_here, expert_count * capacity), jnp.float32)
    for which in range(choices_each):
        selector = jnp.where(matches[which], jnp.bfloat16(1.0), selector)
        gate_table = jnp.where(
            matches[which], router_weights[:, which : which + 1].astype(jnp.float32), gate_table
        )
    gate_send = jnp.sum(gate_table, axis=0).astype(jnp.bfloat16).reshape(expert_count, capacity)
    local_weight = down_weight[0]
    gate_float = gate_preact[0].astype(jnp.float32)
    up_float = up_preact[0].astype(jnp.float32)
    active, slope = silu_parts(gate_float)
    hidden = (active * up_float).astype(jnp.bfloat16)
    contract_rows = (((0,), (0,)), ((), ()))
    contract_cols = (((1,), (1,)), ((), ()))
    whole_weight = lax.all_gather(local_weight, "dp", axis=1, tiled=True)
    outgoing = lax.dot_general(
        selector, output_grad, contract_rows, preferred_element_type=jnp.float32
    )
    outgoing = outgoing.astype(jnp.bfloat16).reshape(expert_count, capacity, -1)
    received, gate_slots = (
        lax.all_to_all(outgoing, "expert", split_axis=0, concat_axis=0, tiled=True),
        lax.all_to_all(gate_send, "expert", split_axis=0, concat_axis=0, tiled=True),
    )
    narrow_rows = received.reshape(expert_count * capacity, -1)
    gate_column = gate_slots.reshape(-1).astype(jnp.float32)[:, None]
    fragment = lax.all_gather(narrow_rows, "tensor", axis=1, tiled=True)
    upstream_sum = lax.dot_general(
        fragment, whole_weight, contract_cols, preferred_element_type=jnp.float32
    )
    scaled = (gate_column * fragment.astype(jnp.float32)).astype(jnp.bfloat16)
    grad_part = lax.dot_general(hidden, scaled, contract_rows, preferred_element_type=jnp.float32)
    grad_weight = grad_part
    upstream, grad_weight = (upstream_sum, grad_weight)
    rounded = lax.optimization_barrier(grad_weight.astype(jnp.bfloat16)).astype(jnp.float32)
    down_grad = lax.psum_scatter(
        rounded.astype(jnp.bfloat16), "dp", scatter_dimension=1, tiled=True
    )
    score = jnp.sum(hidden.astype(jnp.float32) * upstream, axis=1)
    hidden_grad = gate_column * upstream
    gate_grad = (hidden_grad * up_float * slope).astype(jnp.bfloat16)
    up_grad = (hidden_grad * active).astype(jnp.bfloat16)
    summed_scores = lax.psum(score, "tensor")
    returned = lax.all_to_all(
        summed_scores.reshape(expert_count, capacity),
        "expert",
        split_axis=0,
        concat_axis=0,
        tiled=True,
    )
    flat_scores = returned.reshape(-1)
    router_grad = jnp.stack(
        [
            jnp.sum(jnp.where(matches[which], flat_scores[None, :], 0.0), axis=1)
            for which in range(choices_each)
        ],
        axis=1,
    )
    return (gate_grad[None], up_grad[None], down_grad[None], router_grad)


def solution(mesh):
    placed = (
        P(("dp", "expert"), "tensor"),
        P(("dp", "expert"), None),
        P(("dp", "expert"), None),
        P("expert", "dp", "tensor"),
        P("expert", "dp", "tensor"),
        P("expert", "tensor", "dp"),
    )
    return jax.shard_map(
        local,
        mesh=mesh,
        in_specs=placed,
        out_specs=(
            P("expert", "dp", "tensor"),
            P("expert", "dp", "tensor"),
            P("expert", "tensor", "dp"),
            P(("dp", "expert"), None),
        ),
        check_vma=False,
    )
```

profile of v0, /device:TPU:0, one launch (start us, length us, event | category | flops | bytes accessed | tf_op | source)
XLA Modules:
  0.0 914.7 jit_solution(14753980404124492061)
XLA Ops:
  7.2 0.0 all-gather.4.cloned.1.call-start
  7.2 0.9 copy.28
  8.1 0.1 eq.59
  8.2 0.1 eq.55
  8.4 1.2 reduce-window.6
  9.6 0.2 slice_reduce_fusion
  9.8 0.2 reduce-window.9
  10.0 0.1 add_bitcast_fusion
  10.1 0.1 reduce_sum.48
  10.3 0.1 copy.30
  10.3 0.7 multiply_add_fusion
  11.1 0.8 convolution_convert_fusion.1
  11.8 24.2 %all_to_all.20 = bf16[4,192,1024]{2,1,0:T(8,128)(2,1)} all-to-all(bf16[4,192,1024]{2,1,0:T(8,128)(2,1)S(1)} %bitcast.62), channel_id=1, replica_groups=mesh['dp'=2,'expert'=4,'tensor'=4] {'expert'}, dimensions={0} | all-to-all | bytes 3145728 | tf_op jit(solution)/shard_map/all_to_all | solution.py:45
  36.1 0.0 all-gather.6.cloned.1.call-start
  36.1 0.7 all-gather.6.cloned.1.call-update
  36.8 115.6 %all-gather.4.cloned.1.call-done = bf16[768,4096]{1,0:T(8,128)(2,1)} async-done(((bf16[768,1024]{1,0:T(8,128)(2,1)}), bf16[768,4096]{1,0:T(8,128)(2,1)}) %all-gather.4.cloned.1.call-update) | async-done | bytes 6291472 | tf_op jit(solution)/shard_map/all_gather | solution.py:50
  152.4 342.0 %all-gather.6.cloned.1.call-done = bf16[1,3584,4096]{2,1,0:T(8,128)(2,1)} async-done(((bf16[1,3584,2048]{2,1,0:T(8,128)(2,1)}), bf16[1,3584,4096]{2,1,0:T(8,128)(2,1)}) %all-gather.6.cloned.1.call-update) | async-done | bytes 29360144 | tf_op jit(solution)/shard_map/all_gather | solution.py:39
  494.4 34.1 %multiply_reduce_fusion = (f32[768]{0:T(1024)S(1)}, f32[768,3584]{1,0:T(8,128)}) fusion(bf16[1,768,3584]{2,1,0:T(8,128)(2,1)} %param.10, bf16[1,768,3584]{2,1,0:T(8,128)(2,1)} %param.9, bf16[768,4096]{1,0:T(8,128)(2,1)} %all-gather.4.cloned.1.call-done, bf16[1,3584,4096]{2,1,0:T(8,128)(2,1)} %all-gather.6.cloned.1.call-done), kind=kOutput, calls=%fused_computation.17 | convolution fusion | flops 22578855936 | bytes 57674752 | tf_op jit(solution)/shard_map/dot_general | solution.py:51
  528.4 0.1 all_to_all.15
  528.5 12.3 %psum.7 = f32[4,1,192]{2,1,0:T(1,128)} all-reduce(f32[4,1,192]{2,1,0:T(1,128)S(1)} %all_to_all.15), channel_id=1, replica_groups=mesh['dp'=2,'expert'=4,'tensor'=4] {'tensor'}, use_global_device_ids=true, to_apply=%region_6.7 | all-reduce | flops 768 | bytes 6144 | tf_op jit(solution)/shard_map/psum | solution.py:66
  540.8 3.2 all-to-all-start.2
  544.0 0.0 reduce-scatter.2.cloned.1.call-start
  544.1 3.7 all-to-all-done.2
  547.8 0.1 broadcast_in_dim.75
  547.9 0.5 select_reduce_fusion.1
  548.4 0.1 convert_element_type.92
  548.5 6.1 all_to_all.21
  554.6 0.1 reshape.73
  554.7 32.6 %convolution_convert_fusion = bf16[3584,4096]{1,0:T(8,128)(2,1)} fusion(bf16[768,4096]{1,0:T(8,128)(2,1)} %all-gather.4.cloned.1.call-done, f32[768]{0:T(1024)S(1)} %reshape.73, bf16[1,768,3584]{2,1,0:T(8,128)(2,1)} %param.10, bf16[1,768,3584]{2,1,0:T(8,128)(2,1)} %param.9), kind=kOutput, calls=%fused_computation | convolution fusion | flops 22594715648 | bytes 46664704 | tf_op jit(solution)/shard_map/dot_general | solution.py:55
  587.3 0.6 pad_maximum_fusion
  587.9 15.9 %fusion.11 = (bf16[1,768,3584]{2,1,0:T(8,128)(2,1)}, bf16[1,768,3584]{2,1,0:T(8,128)(2,1)}) fusion(f32[768,3584]{1,0:T(8,128)} %get-tuple-element.14, f32[768]{0:T(1024)S(1)} %reshape.73, bf16[1,768,3584]{2,1,0:T(8,128)(2,1)} %param.9, bf16[1,768,3584]{2,1,0:T(8,128)(2,1)} %param.10), kind=kLoop, calls=%fused_computation.20 | loop fusion | flops 44040192 | bytes 33033216 | tf_op jit(solution)/shard_map/broadcast_in_dim | solution.py:82
  603.8 304.3 %reduce-scatter.2.cloned.1.call-done = bf16[3584,2048]{1,0:T(8,128)(2,1)} async-done(((bf16[3584,4096]{1,0:T(8,128)(2,1)}), bf16[3584,2048]{1,0:T(8,128)(2,1)}) %reduce-scatter.2.cloned.1.call-update) | async-done | bytes 14680080 | tf_op jit(solution)/shard_map/reduce_scatter | solution.py:59
  (14 shorter events, 0.1 us)
Async XLA Ops:
  7.2 3.9 copy-start
  7.2 145.2 %all-gather.4.cloned.1.call-start = ((), (), s32[]{:S(2)}) async-start(), calls=%async_computation.4 | async-start | bytes 7864320 | tf_op jit(solution)/shard_map/all_gather | solution.py:50
  36.1 458.3 %all-gather.6.cloned.1.call-start = ((), (), s32[]{:S(2)}) async-start(), calls=%async_computation.6 | async-start | bytes 44040192 | tf_op jit(solution)/shard_map/all_gather | solution.py:39
  36.8 507.3 %copy-start.2 = (bf16[256,2]{0,1:T(2,128)(2,1)S(1)}, bf16[256,2]{0,1:T(2,128)(2,1)}, u32[]{:S(2)}) copy-start(bf16[256,2]{0,1:T(2,128)(2,1)} %param.8) | copy-start | bytes 3076
  540.8 7.0 all-to-all-start.2
  544.0 364.1 %reduce-scatter.2.cloned.1.call-start = ((), (), s32[]{:S(2)}) async-start(), calls=%async_computation.5 | async-start | bytes 44040192 | tf_op jit(solution)/shard_map/reduce_scatter | solution.py:59
  587.9 320.3 %copy-start.1 = (bf16[256,1024]{1,0:T(8,128)(2,1)S(1)}, bf16[256,1024]{1,0:T(8,128)(2,1)}, u32[]{:S(2)}) copy-start(bf16[256,1024]{1,0:T(8,128)(2,1)} %param.6) | copy-start | bytes 1572868
Sparse Core Ops, SparseCore 0:
  36.2 116.1 all-gather.3
  153.9 340.3 all-gather.5
  587.4 320.6 reduce-scatter.1
where the time goes:
time: 915 us
  waiting for transfers between devices  766 us (84%)
  matrix products  67.4 us (7%)
  blocking collectives  42.6 us (5%)
  other arithmetic  19.3 us (2%)
  between operations  13.8 us (2%)
    all_gather x1, waiting for transfers between devices, local(): whole_weight = lax.all_gather(local_weight, 'dp', axis=1, tiled=True)  342 us
    reduce_scatter x1, waiting for transfers between devices, local(): lax.psum_scatter(rounded.astype(jnp.bfloat16), 'dp', scatter_dimension=1,...  304 us
    all_gather x1, waiting for transfers between devices, local(): fragment = lax.all_gather(narrow_rows, 'tensor', axis=1, tiled=True)  116 us
    dot_general x1, matrix products, local(): lax.dot_general(fragment, whole_weight, contract_cols, preferred_element_...  34.1 us
    dot_general x1, matrix products, local(): lax.dot_general(hidden, scaled, contract_rows, preferred_element_type=jnp...  32.6 us
    all_to_all x1, blocking collectives, local(): lax.all_to_all(outgoing, 'expert', split_axis=0, concat_axis=0, tiled=True)  24.2 us
  transfers between devices with their start and end apart: 4, of which 4 were waited for; matrix products, arithmetic and copies ran while one was open for 2% of the time, Pallas kernels for 0%

commit v1 on v0

--- a/solution.py
+++ b/solution.py
@@ -47,7 +47,14 @@
     )
     narrow_rows = received.reshape(expert_count * capacity, -1)
     gate_column = gate_slots.reshape(-1).astype(jnp.float32)[:, None]
-    fragment = lax.all_gather(narrow_rows, "tensor", axis=1, tiled=True)
+    ring = [narrow_rows]
+    for hop in range(3):
+        ring.append(lax.ppermute(ring[-1], "tensor", [(dev, (dev + 1) % 4) for dev in range(4)]))
+    fragment = jnp.roll(
+        jnp.concatenate(ring[::-1], axis=1),
+        (lax.axis_index("tensor") + 1) * ring[0].shape[1],
+        axis=1,
+    )
     upstream_sum = lax.dot_general(
         fragment, whole_weight, contract_cols, preferred_element_type=jnp.float32
     )

time: 915 us -> 776 us (0.85)
  waiting for transfers between devices: 766 us -> 608 us
  local copies, waits for them, and re-layouts: 1.92 us -> 19.5 us
    all_gather x1, waiting for transfers between devices: 342 us -> 190 us  [local(): whole_weight = lax.all_gather(local_weight, 'dp', axis=1, tiled=True)]
    all_gather x1 -> x0, waiting for transfers between devices: 116 us -> none  [local(): fragment = lax.all_gather(narrow_rows, 'tensor', axis=1, tiled=True)]
    ppermute x0 -> x3, waiting for transfers between devices: none -> 109 us  [local(): lax.ppermute(ring[-1], 'tensor', [(dev, (dev + 1) % 4) for dev in range(4)])]
    unnamed x7 -> x20, local copies, waits for them, and re-layouts: 0.88 us -> 17.2 us
  transfers between devices with their start and end apart: 4 -> 6, of which waited for: 4 -> 6; matrix products, arithmetic and copies ran while one was open for 2% -> 5% of each run, Pallas kernels for 0% -> 0%
where the time goes in v1:
time: 776 us; the launch traced here: 775 us
  waiting for transfers between devices  608 us (78%)
  matrix products  67.5 us (9%)
  blocking collectives  42.5 us (5%)
  local copies, waits for them, and re-layouts  19.5 us (3%)
  other arithmetic  18.6 us (2%)
  between operations  14.2 us (2%)
    reduce_scatter x1, waiting for transfers between devices, local(): lax.psum_scatter(rounded.astype(jnp.bfloat16), 'dp', scatter_dimension=1,...  304 us
    all_gather x1, waiting for transfers between devices, local(): whole_weight = lax.all_gather(local_weight, 'dp', axis=1, tiled=True)  190 us
    ppermute x3, waiting for transfers between devices, local(): lax.ppermute(ring[-1], 'tensor', [(dev, (dev + 1) % 4) for dev in range(4)])  109 us
    dot_general x1, matrix products, local(): lax.dot_general(fragment, whole_weight, contract_cols, preferred_element_...  34.1 us
    dot_general x1, matrix products, local(): lax.dot_general(hidden, scaled, contract_rows, preferred_element_type=jnp...  32.6 us
    all_to_all x1, blocking collectives, local(): lax.all_to_all(outgoing, 'expert', split_axis=0, concat_axis=0, tiled=True)  24.1 us
    unnamed x20, local copies, waits for them, and re-layouts  17.2 us
    broadcast_in_dim x1, other arithmetic, local(): return (gate_grad[None], up_grad[None], down_grad[None], router_grad)  15.9 us
  transfers between devices with their start and end apart: 6, of which 6 were waited for; matrix products, arithmetic and copies ran while one was open for 5% of the time, Pallas kernels for 0%

profile of v1, /device:TPU:0, one launch (start us, length us, event | category | flops | bytes accessed | tf_op | source)
XLA Modules:
  0.0 775.2 jit_solution(15555246217838544934)
XLA Ops:
  7.2 0.7 all-gather.3.cloned.1.call-update
  8.1 0.1 eq.62
  8.4 1.2 reduce-window.6
  9.6 0.2 slice_reduce_fusion
  9.8 0.2 reduce-window.9
  10.1 0.1 reduce_sum.48
  10.4 0.8 convolution_convert_fusion.1
  11.1 24.1 %all_to_all.20 = bf16[4,192,1024]{2,1,0:T(8,128)(2,1)S(1)} all-to-all(bf16[4,192,1024]{2,1,0:T(8,128)(2,1)S(1)} %bitcast.63), channel_id=1, replica_groups=mesh['dp'=2,'expert'=4,'tensor'=4] {'expert'}, dimensions={0} | all-to-all | bytes 3145728 | tf_op jit(solution)/shard_map/all_to_all | solution.py:45
  35.2 1.6 collective-permute-start
  36.8 36.1 %collective-permute-done = bf16[768,1024]{1,0:T(8,128)(2,1)S(1)} collective-permute-done((bf16[768,1024]{1,0:T(8,128)(2,1)S(1)}, bf16[768,1024]{1,0:T(8,128)(2,1)S(1)}, u32[]{:S(2)}, u32[]{:S(2)}) %collective-permute-start) | collective-permute-done | bytes 1572896 | tf_op jit(solution)/shard_map/ppermute | solution.py:52
  72.9 1.1 copy-done.2
  74.0 36.8 %collective-permute-done.1 = bf16[768,1024]{1,0:T(8,128)(2,1)} collective-permute-done((bf16[768,1024]{1,0:T(8,128)(2,1)S(1)}, bf16[768,1024]{1,0:T(8,128)(2,1)}, u32[]{:S(2)}, u32[]{:S(2)}) %collective-permute-start.1) | collective-permute-done | bytes 1572896 | tf_op jit(solution)/shard_map/ppermute | solution.py:52
  110.9 36.1 %collective-permute-done.2 = bf16[768,1024]{1,0:T(8,128)(2,1)} collective-permute-done((bf16[768,1024]{1,0:T(8,128)(2,1)}, bf16[768,1024]{1,0:T(8,128)(2,1)}, u32[]{:S(2)}, u32[]{:S(2)}) %collective-permute-start.2) | collective-permute-done | bytes 1572896 | tf_op jit(solution)/shard_map/ppermute | solution.py:52
  147.0 2.7 constant_dynamic-update-slice_fusion.7
  149.6 2.7 constant_dynamic-update-slice_fusion.6
  152.3 2.7 constant_dynamic-update-slice_fusion.5
  155.0 1.3 constant_dynamic-update-slice_fusion.4
  156.2 2.7 constant_dynamic-update-slice_fusion.3
  158.9 2.7 constant_dynamic-update-slice_fusion.2
  161.6 1.3 constant_dynamic-update-slice_fusion.1
  162.8 1.3 constant_dynamic-update-slice_fusion
  164.1 190.5 %all-gather.3.cloned.1.call-done = bf16[1,3584,4096]{2,1,0:T(8,128)(2,1)} async-done(((bf16[1,3584,2048]{2,1,0:T(8,128)(2,1)}), bf16[1,3584,4096]{2,1,0:T(8,128)(2,1)}) %all-gather.3.cloned.1.call-update) | async-done | bytes 29360144 | tf_op jit(solution)/shard_map/all_gather | solution.py:39
  354.5 34.1 %multiply_reduce_fusion = (f32[768]{0:T(1024)S(1)}, f32[768,3584]{1,0:T(8,128)}) fusion(bf16[1,768,3584]{2,1,0:T(8,128)(2,1)} %param.10, bf16[1,768,3584]{2,1,0:T(8,128)(2,1)} %param.9, bf16[1,3584,4096]{2,1,0:T(8,128)(2,1)} %all-gather.3.cloned.1.call-done, bf16[768,8192]{1,0:T(8,128)(2,1)} %constant_dynamic-update-slice_fusion, s32[]{:T(128)S(6)} %select_n.39), kind=kOutput, calls=%fused_computation.17 | convolution fusion | flops 22578855936 | bytes 57674756 | tf_op jit(solution)/shard_map/dot_general | solution.py:58
  388.7 12.2 %psum.7 = f32[4,1,192]{2,1,0:T(1,128)} all-reduce(f32[4,1,192]{2,1,0:T(1,128)S(1)} %all_to_all.15), channel_id=1, replica_groups=mesh['dp'=2,'expert'=4,'tensor'=4] {'tensor'}, use_global_device_ids=true, to_apply=%region_6.7 | all-reduce | flops 768 | bytes 6144 | tf_op jit(solution)/shard_map/psum | solution.py:73
  400.9 3.2 all-to-all-start.2
  404.3 3.7 all-to-all-done.2
  408.1 0.5 select_reduce_fusion.1
  408.6 6.1 all_to_all.21
  414.9 32.6 %convolution_convert_fusion = bf16[3584,4096]{1,0:T(8,128)(2,1)} fusion(f32[768]{0:T(1024)S(1)} %reshape.73, bf16[768,8192]{1,0:T(8,128)(2,1)} %constant_dynamic-update-slice_fusion, s32[]{:T(128)S(6)} %select_n.39, bf16[1,768,3584]{2,1,0:T(8,128)(2,1)} %param.10, bf16[1,768,3584]{2,1,0:T(8,128)(2,1)} %param.9), kind=kOutput, calls=%fused_computation | convolution fusion | flops 22594715648 | bytes 46664708 | tf_op jit(solution)/shard_map/dot_general | solution.py:62
  447.5 0.6 pad_maximum_fusion
  448.1 15.9 %fusion.13 = (bf16[1,768,3584]{2,1,0:T(8,128)(2,1)}, bf16[1,768,3584]{2,1,0:T(8,128)(2,1)}) fusion(f32[768,3584]{1,0:T(8,128)} %get-tuple-element.14, f32[768]{0:T(1024)S(1)} %reshape.73, bf16[1,768,3584]{2,1,0:T(8,128)(2,1)} %param.9, bf16[1,768,3584]{2,1,0:T(8,128)(2,1)} %param.10), kind=kLoop, calls=%fused_computation.22 | loop fusion | flops 44040192 | bytes 33033216 | tf_op jit(solution)/shard_map/broadcast_in_dim | solution.py:89
  464.0 304.3 %reduce-scatter.2.cloned.1.call-done = bf16[3584,2048]{1,0:T(8,128)(2,1)} async-done(((bf16[3584,4096]{1,0:T(8,128)(2,1)}), bf16[3584,2048]{1,0:T(8,128)(2,1)}) %reduce-scatter.2.cloned.1.call-update) | async-done | bytes 14680080 | tf_op jit(solution)/shard_map/reduce_scatter | solution.py:66
  (31 shorter events, 1.0 us)
Async XLA Ops:
  7.2 3.2 copy-start
  7.2 0.7 copy-start.4
  7.2 347.4 %all-gather.3.cloned.1.call-start = ((), (), s32[]{:S(2)}) async-start(), calls=%async_computation.5 | async-start | bytes 44040192 | tf_op jit(solution)/shard_map/all_gather | solution.py:39
  35.2 37.6 %collective-permute-start = (bf16[768,1024]{1,0:T(8,128)(2,1)S(1)}, bf16[768,1024]{1,0:T(8,128)(2,1)S(1)}, u32[]{:S(2)}, u32[]{:S(2)}) collective-permute-start(bf16[768,1024]{1,0:T(8,128)(2,1)S(1)} %bitcast.60), channel_id=1, source_target_pairs={{0,1},{1,2},{2,3},{3,0},{4,5},{5,6},{6,7},{7,4},{8,9},{9,10},{10,1... | collective-permute-start | bytes 4718600 | tf_op jit(solution)/shard_map/ppermute | solution.py:52
  72.9 1.1 copy-start.2
  74.0 36.8 %collective-permute-start.1 = (bf16[768,1024]{1,0:T(8,128)(2,1)S(1)}, bf16[768,1024]{1,0:T(8,128)(2,1)}, u32[]{:S(2)}, u32[]{:S(2)}) collective-permute-start(bf16[768,1024]{1,0:T(8,128)(2,1)S(1)} %collective-permute-done), channel_id=1, source_target_pairs={{0,1},{1,2},{2,3},{3,0},{4,5},{5,6},{6,7},{7,4},{8,9},{9,10},{10,1... | collective-permute-start | bytes 4718600 | tf_op jit(solution)/shard_map/ppermute | solution.py:52
  110.8 36.1 %collective-permute-start.2 = (bf16[768,1024]{1,0:T(8,128)(2,1)}, bf16[768,1024]{1,0:T(8,128)(2,1)}, u32[]{:S(2)}, u32[]{:S(2)}) collective-permute-start(bf16[768,1024]{1,0:T(8,128)(2,1)} %collective-permute-done.1), channel_id=1, source_target_pairs={{0,1},{1,2},{2,3},{3,0},{4,5},{5,6},{6,7},{7,4},{8,9},{9,10},{10,1... | collective-permute-start | bytes 4718600 | tf_op jit(solution)/shard_map/ppermute | solution.py:52
  110.8 50.7 %copy-start.3 = (bf16[768,1024]{1,0:T(8,128)(2,1)S(1)}, bf16[768,1024]{1,0:T(8,128)(2,1)}, u32[]{:S(2)}) copy-start(bf16[768,1024]{1,0:T(8,128)(2,1)} %copy-done.2) | copy-start | bytes 4718596
  164.1 240.2 %copy-start.5 = (bf16[256,2]{0,1:T(2,128)(2,1)S(1)}, bf16[256,2]{0,1:T(2,128)(2,1)}, u32[]{:S(2)}) copy-start(bf16[256,2]{0,1:T(2,128)(2,1)} %param.8) | copy-start | bytes 3076
  400.9 7.0 all-to-all-start.2
  404.2 364.1 %reduce-scatter.2.cloned.1.call-start = ((), (), s32[]{:S(2)}) async-start(), calls=%async_computation.4 | async-start | bytes 44040192 | tf_op jit(solution)/shard_map/reduce_scatter | solution.py:66
  448.1 320.3 %copy-start.1 = (bf16[256,1024]{1,0:T(8,128)(2,1)S(1)}, bf16[256,1024]{1,0:T(8,128)(2,1)}, u32[]{:S(2)}) copy-start(bf16[256,1024]{1,0:T(8,128)(2,1)} %param.6) | copy-start | bytes 1572868
Sparse Core Ops, SparseCore 0:
  9.6 344.9 all-gather.2
  447.6 320.6 reduce-scatter.1
